TPU v7x, 512 devices: a whole 4x8x8 slice. The times are simulated.
512 devices in a mesh: panel: 64 (over y, z), point: 8 (over x, core).
Axes of the slice: x: 4, y: 8, z: 8, core: 2. Of those that a mesh axis runs over, the one named last changes fastest.
Arguments:
- node_velocity: float32 [2, 1048576], P(None, ('panel', 'point')), may hold values from -1.5 to 1.5
- node_owner: int32 [1048576, 1], P(('panel', 'point')), may hold values from 0 to 63; in each aligned block of 2048 rows (0 to 2047, 2048 to 4095, ...) at most 64 rows name the same one
- node_panel: int32 [1048576], P(('panel', 'point')), may hold values from 0 to 127
- panel_centroid: float32 [3, 8192], P(None, 'panel'), may hold values from -1 to 1
- panel_area: float32 [8192], P('panel'), may hold values from 0.05 to 0.5
- field_points: float32 [3, 65536], P(None, ('panel', 'point')), may hold values from 1.2 to 3
Outputs:
- pressure: float32 [2, 65536], P(None, ('panel', 'point'))
Inputs may be any that keep to these rules, and one draw needn't show every extreme that they name: `node_owner`: among the rows of one device at most 64 name the same owner, a bound that some block reaches.
All inputs are finite; a program needn't handle non-finite values.
Results may differ from a plain program's by a relative error of at most 0.0003.
Values sent between devices are 32-bit elements; how exact they have to be, the bound alone decides.
No kernel may reach another device: no remote copies, remote signals or barrier semaphores. Data moves between devices by JAX's collectives and lax.ppermute only.
A program may use at most 64 MiB of HBM per device.

v0:
```python
import math

import jax
import jax.numpy as jnp
from jax import lax
from jax.sharding import PartitionSpec as P

WAVENUMBER = 40.0
FOUR_PI = 4.0 * math.pi


def green_block(centers, strength, points):
    delta_x = points[0][None, :] - centers[0][:, None]
    delta_y = points[1][None, :] - centers[1][:, None]
    delta_z = points[2][None, :] - centers[2][:, None]
    distance = jnp.sqrt(delta_x * delta_x + delta_y * delta_y + delta_z * delta_z)
    inverse = 1.0 / (FOUR_PI * distance)
    phase_angle = WAVENUMBER * distance
    cosine_part = jnp.cos(phase_angle) * inverse
    sine_part = jnp.sin(phase_angle) * inverse
    with_cosine = jnp.dot(
        strength, cosine_part, precision=lax.Precision.HIGHEST, preferred_element_type=jnp.float32
    )
    with_sine = jnp.dot(
        strength, sine_part, precision=lax.Precision.HIGHEST, preferred_element_type=jnp.float32
    )
    return jnp.stack([with_cosine[0] - with_sine[1], with_sine[0] + with_cosine[1]])


def green_points(centers, strength, points):
    width_now = points.shape[1]
    block_size = 2048
    block_count = width_now // block_size
    grouped = points.reshape(3, block_count, block_size).transpose(1, 0, 2)
    result = lax.map(lambda single: green_block(centers, strength, single), grouped)
    return result.transpose(1, 0, 2).reshape(2, width_now)


def shards(node_velocity, node_owner, node_panel, panel_centroid, panel_area, field_points):
    row_count = node_panel.shape[0]
    slab_count = lax.axis_size("panel")
    capacity = max(2 * row_count // slab_count, 2)
    panel_count = panel_area.shape[0]
    destination = node_owner[:, 0]
    one_hot = (destination[:, None] == jnp.arange(slab_count, dtype=jnp.int32)[None, :]).astype(
        jnp.int32
    )
    earlier = jnp.cumsum(one_hot, axis=0) - one_hot
    position_in = jnp.sum(earlier * one_hot, axis=1)
    send_slot = destination * capacity + position_in
    sent_velocity = (
        jnp.zeros((2, slab_count * capacity), jnp.float32).at[:, send_slot].set(node_velocity)
    )
    sent_velocity = sent_velocity.reshape(2, slab_count, capacity)
    sent_panels = (
        jnp.full((1, slab_count * capacity), -1, jnp.int32).at[0, send_slot].set(node_panel)
    )
    sent_panels = sent_panels.reshape(1, slab_count, capacity)
    got_velocity, got_panels = (
        lax.all_to_all(sent_velocity, "panel", split_axis=1, concat_axis=1, tiled=True),
        lax.all_to_all(sent_panels, "panel", split_axis=1, concat_axis=1, tiled=True),
    )
    members = (
        got_panels.reshape(1, -1) == jnp.arange(panel_count, dtype=jnp.int32)[:, None]
    ).astype(jnp.float32)
    partial_value = jnp.dot(
        got_velocity.reshape(2, -1),
        members.T,
        precision=lax.Precision.HIGHEST,
        preferred_element_type=jnp.float32,
    )
    velocity = lax.psum(partial_value, "point")
    strength = jnp.stack([-panel_area * velocity[1], panel_area * velocity[0]])
    terms = green_points(
        panel_centroid, strength, lax.all_gather(field_points, "panel", axis=1, tiled=True)
    )
    pressure = lax.psum_scatter(terms, "panel", scatter_dimension=1, tiled=True)
    return pressure


def solution(mesh):
    return jax.shard_map(
        shards,
        mesh=mesh,
        in_specs=(
            P(None, ("panel", "point")),
            P(("panel", "point"), None),
            P(("panel", "point")),
            P(None, "panel"),
            P("panel"),
            P(None, ("panel", "point")),
        ),
        out_specs=P(None, ("panel", "point")),
        check_vma=False,
    )
```

profile of v0, /device:TPU:1, one launch (start us, length us, event | category | flops | bytes accessed | tf_op | source)
XLA Modules:
  0.0 431.4 jit_solution(8571895491091171147)
XLA Ops:
  6.5 0.8 fusion.35
  7.4 18.1 %reduce-window.6 = s32[64,16,128]{2,1,0:T(8,128)S(1)} reduce-window(s32[64,16,128]{2,1,0:T(8,128)S(1)} %fusion.35, s32[]{:T(128)} %constant.5.clone.1), window={size=1x1x128 pad=0_0x0_0x127_0}, to_apply=%region_0.0 | reduce-window | flops 16646144 | bytes 1048580 | tf_op jit(solution)/shard_map/reduce-window
  25.7 0.4 copy.24
  26.6 0.3 fusion.34
  27.1 8.2 %scatter_custom_fusion.1 = s32[4096]{0:T(1024)S(1)} fusion(s32[2048]{0:T(1024)S(1)} %broadcast_select_fusion, s32[2048]{0:T(1024)} %param.10, s32[]{:T(128)} %constant.22.clone.1), kind=kCustom, calls=%fused_computation.58 | custom fusion | bytes 16896
  35.3 0.7 reshape.47
  36.0 17.1 %all-to-all-start.1 = ((s32[1,64,64]{2,0,1:T(1,128)}), s32[1,64,64]{2,0,1:T(1,128)S(1)}, u32[]{:S(2)}, u32[]{:S(2)}) async-start(s32[1,64,64]{2,0,1:T(1,128)} %reshape.47), calls=%async_computation.1 | async-start | bytes 65536 | tf_op jit(solution)/shard_map/all_to_all | solution.py:61
  53.2 0.4 copy.20
  53.5 6.1 %scatter_custom_fusion = f32[2,4096]{0,1:T(8,128)S(1)} fusion(s32[2048]{0:T(1024)S(1)} %bitcast.105, f32[2048,2]{1,0:T(8,128)S(1)} %copy.20, f32[]{:T(128)} %constant.6.clone.1), kind=kCustom, calls=%fused_computation.44 | custom fusion | bytes 32772 | tf_op jit(solution)/shard_map/scatter | solution.py:52
  59.7 0.7 copy.21
  60.4 0.7 reshape.83
  61.1 2.9 all-to-all-done.1
  64.0 9.2 %all-to-all-start = ((f32[64,1,128]{2,1,0:T(1,128)}), f32[64,1,128]{2,1,0:T(1,128)S(1)}, u32[]{:S(2)}, u32[]{:S(2)}) async-start(f32[64,1,128]{2,1,0:T(1,128)} %reshape.83), calls=%async_computation | async-start | bytes 65536 | tf_op jit(solution)/shard_map/all_to_all | solution.py:60
  73.3 37.3 %all_gather.3 = f32[3,8192]{1,0:T(4,128)S(1)} all-gather(f32[3,128]{1,0:T(4,128)S(1)} %copy-done.3), channel_id=1, replica_groups=mesh['panel'=64,'point'=8] {'panel'}, dimensions={1}, use_global_device_ids=true | all-gather | bytes 99840 | tf_op jit(solution)/shard_map/all_gather | solution.py:75
  110.6 0.5 broadcast.81
  111.1 0.7 reduce.7
  111.9 0.6 broadcast.82
  112.5 0.8 reduce.8
  113.5 1.0 fusion.28
  114.5 26.0 %psum.7 = f32[2,128]{1,0:T(2,128)S(1)} all-reduce(f32[2,128]{1,0:T(2,128)S(1)} %fusion.28), channel_id=1, replica_groups=mesh['panel'=64,'point'=8] {'point'}, use_global_device_ids=true, to_apply=%region_5.6 | all-reduce | flops 256 | bytes 2048 | tf_op jit(solution)/shard_map/psum | solution.py:72
  140.6 38.7 %while.10 = (s32[]{:T(128)}, f32[4,2,2048]{2,1,0:T(2,128)S(1)}, f32[4,3,2048]{2,1,0:T(4,128)S(1)}, f32[3,128]{1,0:T(4,128)S(1)}, f32[2,128]{1,0:T(2,128)S(1)}, /*index=5*/s32[]{:T(128)}, s32[]{:T(128)}, s32[]{}, s32[]{}) while((s32[]{:T(128)}, f32[4,2,2048]{2,1,0:T(2,128)S(1)}, f32[4,3,2048]{2,1,0:T(4,128)S(1)}, f32[3,128]{1,0:T(4,128)S(1)}, ...), condition=%wide.region_7.8_spmd, body=%wide.region_6.7_spmd.sunk | while | flops 18882564 | bytes 221325 | solution.py:35
  140.7 4.7 %convolution_bitcast_fusion.5 = f32[2,2048]{1,0:T(2,128)S(1)} fusion(f32[2,128]{1,0:T(2,128)S(1)} %get-tuple-element.122, f32[128]{0:T(128)S(1)} %get-tuple-element.92, f32[2048]{0:T(1024)S(1)} %bitcast.99, f32[128]{0:T(128)S(1)} %get-tuple-element.94, f32[2048]{0:T(1024)S(1)} %bitcast.97, f32[128]{0:T(128)S(1)} %get-tuple-element.96, ...), kind=kOutput, calls=%fused_computation.3.clone.1 | convolution fusion | flops 9437184 | bytes 43520 | tf_op jit(solution)/shard_map/while/body/eval_jaxpr/dot_general | solution.py:21
  145.4 4.8 %convolution_bitcast_fusion.4 = f32[2,2048]{1,0:T(2,128)S(1)} fusion(f32[2,128]{1,0:T(2,128)S(1)} %get-tuple-element.122, f32[128]{0:T(128)S(1)} %get-tuple-element.92, f32[2048]{0:T(1024)S(1)} %bitcast.100, f32[128]{0:T(128)S(1)} %get-tuple-element.94, f32[2048]{0:T(1024)S(1)} %bitcast.98, f32[128]{0:T(128)S(1)} %get-tuple-element.96, ...), kind=kOutput, calls=%fused_computation.2.clone.1 | convolution fusion | flops 9437184 | bytes 43520 | tf_op jit(solution)/shard_map/while/body/eval_jaxpr/dot_general | solution.py:24
  150.3 4.7 %convolution_bitcast_fusion.5 = f32[2,2048]{1,0:T(2,128)S(1)} fusion(f32[2,128]{1,0:T(2,128)S(1)} %get-tuple-element.122, f32[128]{0:T(128)S(1)} %get-tuple-element.92, f32[2048]{0:T(1024)S(1)} %bitcast.99, f32[128]{0:T(128)S(1)} %get-tuple-element.94, f32[2048]{0:T(1024)S(1)} %bitcast.97, f32[128]{0:T(128)S(1)} %get-tuple-element.96, ...), kind=kOutput, calls=%fused_computation.3.clone.1 | convolution fusion | flops 9437184 | bytes 43520 | tf_op jit(solution)/shard_map/while/body/eval_jaxpr/dot_general | solution.py:21
  155.1 4.8 %convolution_bitcast_fusion.4 = f32[2,2048]{1,0:T(2,128)S(1)} fusion(f32[2,128]{1,0:T(2,128)S(1)} %get-tuple-element.122, f32[128]{0:T(128)S(1)} %get-tuple-element.92, f32[2048]{0:T(1024)S(1)} %bitcast.100, f32[128]{0:T(128)S(1)} %get-tuple-element.94, f32[2048]{0:T(1024)S(1)} %bitcast.98, f32[128]{0:T(128)S(1)} %get-tuple-element.96, ...), kind=kOutput, calls=%fused_computation.2.clone.1 | convolution fusion | flops 9437184 | bytes 43520 | tf_op jit(solution)/shard_map/while/body/eval_jaxpr/dot_general | solution.py:24
  160.0 4.7 %convolution_bitcast_fusion.5 = f32[2,2048]{1,0:T(2,128)S(1)} fusion(f32[2,128]{1,0:T(2,128)S(1)} %get-tuple-element.122, f32[128]{0:T(128)S(1)} %get-tuple-element.92, f32[2048]{0:T(1024)S(1)} %bitcast.99, f32[128]{0:T(128)S(1)} %get-tuple-element.94, f32[2048]{0:T(1024)S(1)} %bitcast.97, f32[128]{0:T(128)S(1)} %get-tuple-element.96, ...), kind=kOutput, calls=%fused_computation.3.clone.1 | convolution fusion | flops 9437184 | bytes 43520 | tf_op jit(solution)/shard_map/while/body/eval_jaxpr/dot_general | solution.py:21
  164.7 4.8 %convolution_bitcast_fusion.4 = f32[2,2048]{1,0:T(2,128)S(1)} fusion(f32[2,128]{1,0:T(2,128)S(1)} %get-tuple-element.122, f32[128]{0:T(128)S(1)} %get-tuple-element.92, f32[2048]{0:T(1024)S(1)} %bitcast.100, f32[128]{0:T(128)S(1)} %get-tuple-element.94, f32[2048]{0:T(1024)S(1)} %bitcast.98, f32[128]{0:T(128)S(1)} %get-tuple-element.96, ...), kind=kOutput, calls=%fused_computation.2.clone.1 | convolution fusion | flops 9437184 | bytes 43520 | tf_op jit(solution)/shard_map/while/body/eval_jaxpr/dot_general | solution.py:24
  169.7 4.7 %convolution_bitcast_fusion.5 = f32[2,2048]{1,0:T(2,128)S(1)} fusion(f32[2,128]{1,0:T(2,128)S(1)} %get-tuple-element.122, f32[128]{0:T(128)S(1)} %get-tuple-element.92, f32[2048]{0:T(1024)S(1)} %bitcast.99, f32[128]{0:T(128)S(1)} %get-tuple-element.94, f32[2048]{0:T(1024)S(1)} %bitcast.97, f32[128]{0:T(128)S(1)} %get-tuple-element.96, ...), kind=kOutput, calls=%fused_computation.3.clone.1 | convolution fusion | flops 9437184 | bytes 43520 | tf_op jit(solution)/shard_map/while/body/eval_jaxpr/dot_general | solution.py:21
  174.4 4.8 %convolution_bitcast_fusion.4 = f32[2,2048]{1,0:T(2,128)S(1)} fusion(f32[2,128]{1,0:T(2,128)S(1)} %get-tuple-element.122, f32[128]{0:T(128)S(1)} %get-tuple-element.92, f32[2048]{0:T(1024)S(1)} %bitcast.100, f32[128]{0:T(128)S(1)} %get-tuple-element.94, f32[2048]{0:T(1024)S(1)} %bitcast.98, f32[128]{0:T(128)S(1)} %get-tuple-element.96, ...), kind=kOutput, calls=%fused_computation.2.clone.1 | convolution fusion | flops 9437184 | bytes 43520 | tf_op jit(solution)/shard_map/while/body/eval_jaxpr/dot_general | solution.py:24
  179.3 2.6 copy.25
  181.9 241.1 %reduce-scatter.4.cloned.1.call-done = f32[128,2]{1,0:T(8,128)} async-done(((f32[8192,2]{1,0:T(8,128)}), f32[128,2]{1,0:T(8,128)}) %reduce-scatter.4.cloned.1.call-update) | async-done | bytes 1040
  423.1 1.5 copy.26
  (47 shorter events, 1.6 us)
Async XLA Ops:
  6.5 20.0 %copy-start = (s32[2048,1]{0,1:T(1,128)S(1)}, s32[2048,1]{0,1:T(1,128)}, u32[]{:S(2)}) copy-start(s32[2048,1]{0,1:T(1,128)} %param.9) | copy-start | bytes 24580
  7.3 19.5 %copy-start.6 = (s32[2]{0:T(128)S(1)}, s32[2]{0:T(128)}, u32[]{:S(2)}) copy-start(s32[2]{0:T(128)} %constant.38) | copy-start | bytes 28
  7.4 19.6 %copy-start.5 = (s32[2]{0:T(128)S(1)}, s32[2]{0:T(128)}, u32[]{:S(2)}) copy-start(s32[2]{0:T(128)} %constant.35) | copy-start | bytes 28
  7.4 45.8 %copy-start.2 = (f32[2,2048]{1,0:T(2,128)S(1)}, f32[2,2048]{1,0:T(2,128)}, u32[]{:S(2)}) copy-start(f32[2,2048]{1,0:T(2,128)} %param.8) | copy-start | bytes 49156
  36.0 28.0 %all-to-all-start.1 = ((s32[1,64,64]{2,0,1:T(1,128)}), s32[1,64,64]{2,0,1:T(1,128)S(1)}, u32[]{:S(2)}, u32[]{:S(2)}) async-start(s32[1,64,64]{2,0,1:T(1,128)} %reshape.47), calls=%async_computation.1 | async-start | bytes 65536 | tf_op jit(solution)/shard_map/all_to_all | solution.py:61
  53.5 19.8 %copy-start.3 = (f32[3,128]{1,0:T(4,128)S(1)}, f32[3,128]{1,0:T(4,128)}, u32[]{:S(2)}) copy-start(f32[3,128]{1,0:T(4,128)} %param.13) | copy-start | bytes 4612
  59.6 80.9 %copy-start.4 = (f32[128]{0:T(128)S(1)}, f32[128]{0:T(128)}, u32[]{:S(2)}) copy-start(f32[128]{0:T(128)} %param.12) | copy-start | bytes 1540
  59.7 80.9 %copy-start.1 = (f32[3,128]{1,0:T(4,128)S(1)}, f32[3,128]{1,0:T(4,128)}, u32[]{:S(2)}) copy-start(f32[3,128]{1,0:T(4,128)} %param.11) | copy-start | bytes 4612
  64.0 47.9 %all-to-all-start = ((f32[64,1,128]{2,1,0:T(1,128)}), f32[64,1,128]{2,1,0:T(1,128)S(1)}, u32[]{:S(2)}, u32[]{:S(2)}) async-start(f32[64,1,128]{2,1,0:T(1,128)} %reshape.83), calls=%async_computation | async-start | bytes 65536 | tf_op jit(solution)/shard_map/all_to_all | solution.py:60
  73.2 349.8 %reduce-scatter.4.cloned.1.call-start = ((), (), s32[]{:S(2)}) async-start(), calls=%async_computation.3 | async-start | bytes 4259840
Sparse Core Ops, SparseCore 0:
  182.0 240.9 reduce-scatter.3
where the time goes:
time: 436 us; the launch traced here: 431 us
  waiting for transfers between devices  244 us (56%)
  blocking collectives  63.3 us (15%)
  matrix products  39.2 us (9%)
  starting transfers between devices  26.4 us (6%)
  local copies, waits for them, and re-layouts  23.1 us (5%)
  other arithmetic  21.5 us (5%)
  between operations  13.6 us (3%)
    unnamed x2, waiting for transfers between devices  241 us
    all_gather x1, blocking collectives, shards(): lax.all_gather(field_points, 'panel', axis=1, tiled=True)  37.3 us
    psum x1, blocking collectives, shards(): velocity = lax.psum(partial_value, 'point')  26 us
    dot_general x4, matrix products, green_block(): jnp.dot(strength, sine_part, precision=lax.Precision.HIGHEST, preferred_e...  19.2 us
    dot_general x4, matrix products, green_block(): jnp.dot(strength, cosine_part, precision=lax.Precision.HIGHEST, preferred...  19 us
    another operation x3, other arithmetic  18.5 us
    all_to_all x1, starting transfers between devices, shards(): lax.all_to_all(sent_panels, 'panel', split_axis=1, concat_axis=1, tiled=T...  17.1 us
    unnamed x20, local copies, waits for them, and re-layouts  13.6 us
  transfers between devices with their start and end apart: 3, of which 2 were waited for; matrix products, arithmetic and copies ran while one was open for 2% of the time, Pallas kernels for 0%

commit v1 on v0

v1 whole, which is shorter than its diff:
```python
import math

import jax
import jax.numpy as jnp
from jax import lax
from jax.sharding import PartitionSpec as P

WAVENUMBER = 40.0
FOUR_PI = 4.0 * math.pi


def green_points(centers, strength, points):
    delta_x = points[0][None, :] - centers[0][:, None]
    delta_y = points[1][None, :] - centers[1][:, None]
    delta_z = points[2][None, :] - centers[2][:, None]
    distance = jnp.sqrt(delta_x * delta_x + delta_y * delta_y + delta_z * delta_z)
    inverse = 1.0 / (FOUR_PI * distance)
    phase_angle = WAVENUMBER * distance
    cosine_part = jnp.cos(phase_angle) * inverse
    sine_part = jnp.sin(phase_angle) * inverse
    real = strength[0][:, None] * cosine_part - strength[1][:, None] * sine_part
    imag = strength[0][:, None] * sine_part + strength[1][:, None] * cosine_part
    return jnp.stack([jnp.sum(real, axis=0), jnp.sum(imag, axis=0)])


def shards(node_velocity, node_owner, node_panel, panel_centroid, panel_area, field_points):
    slab_count = lax.axis_size("panel")
    slab_width = panel_area.shape[0]
    destination = node_owner[:, 0]
    owner_hot = (destination[None, :] == jnp.arange(slab_count, dtype=jnp.int32)[:, None]).astype(
        jnp.float32
    )
    weighted = (node_velocity[:, None, :] * owner_hot[None, :, :]).reshape(2 * slab_count, -1)
    panel_hot = (node_panel[:, None] == jnp.arange(slab_width, dtype=jnp.int32)[None, :]).astype(
        jnp.float32
    )
    partial = jnp.dot(
        weighted, panel_hot, precision=lax.Precision.HIGHEST, preferred_element_type=jnp.float32
    )
    partial = partial.reshape(2, slab_count, slab_width).transpose(1, 0, 2)
    got = lax.all_to_all(partial, "panel", split_axis=0, concat_axis=0, tiled=True)
    velocity = lax.psum(jnp.sum(got, axis=0), "point")
    strength = jnp.stack([-panel_area * velocity[1], panel_area * velocity[0]])
    packed = jnp.concatenate([strength, panel_centroid], axis=0)
    spread = jnp.broadcast_to(packed[None], (slab_count,) + packed.shape)
    gathered = lax.all_to_all(spread, "panel", split_axis=0, concat_axis=0, tiled=True)
    every = gathered.transpose(1, 0, 2).reshape(packed.shape[0], -1)
    return green_points(every[2:5], every[0:2], field_points)


def solution(mesh):
    return jax.shard_map(
        shards,
        mesh=mesh,
        in_specs=(
            P(None, ("panel", "point")),
            P(("panel", "point"), None),
            P(("panel", "point")),
            P(None, "panel"),
            P("panel"),
            P(None, ("panel", "point")),
        ),
        out_specs=P(None, ("panel", "point")),
        check_vma=False,
    )
```

time: 436 us -> 82.7 us (0.19)
  waiting for transfers between devices: 244 us -> 12.5 us
  matrix products: 39.2 us -> 0.86 us
  local copies, waits for them, and re-layouts: 23.1 us -> 0.91 us
  starting transfers between devices: 26.4 us -> 4.62 us
  blocking collectives: 63.3 us -> 41.9 us
  between operations: 13.6 us -> 0.11 us
    unnamed x2 -> x0, waiting for transfers between devices: 241 us -> none
    dot_general x9 -> x1, matrix products: 39.2 us -> 0.86 us  [shards(): jnp.dot(weighted, panel_hot, precision=lax.Precision.HIGHEST, preferred_e...]
    all_gather x1 -> x0, blocking collectives: 37.3 us -> none  [shards(): lax.all_gather(field_points, 'panel', axis=1, tiled=True)]
    all_to_all x0 -> x1, blocking collectives: none -> 28.1 us  [shards(): lax.all_to_all(partial, 'panel', split_axis=0, concat_axis=0, tiled=True)]
    all_to_all x2 -> x1, starting transfers between devices: 26.4 us -> 4.62 us  [shards(): lax.all_to_all(spread, 'panel', split_axis=0, concat_axis=0, tiled=True)]
    reduce_sum x1 -> x2, other arithmetic: 0.26 us -> 19.4 us  [the longest x1 19.3 us: green_points(): return jnp.stack([jnp.sum(real, axis=0), jnp.sum(imag, axis=0)])]
    another operation x3 -> x1, other arithmetic: 18.5 us -> 0.58 us  [green_points(): return jnp.stack([jnp.sum(real, axis=0), jnp.sum(imag, axis=0)])]
    unnamed x20 -> x10, local copies, waits for them, and re-layouts: 13.6 us -> 0.03 us
  transfers between devices with their start and end apart: 3 -> 1, of which waited for: 2 -> 1; matrix products, arithmetic and copies ran while one was open for 2% -> 0% of each run, Pallas kernels for 0% -> 0%
where the time goes in v1:
time: 82.7 us; the launch traced here: 81.6 us
  blocking collectives  41.9 us (51%)
  other arithmetic  20.7 us (25%)
  waiting for transfers between devices  12.5 us (15%)
  starting transfers between devices  4.62 us (6%)
  local copies, waits for them, and re-layouts  0.91 us (1%)
  matrix products  0.86 us (1%)
    all_to_all x1, blocking collectives, shards(): lax.all_to_all(partial, 'panel', split_axis=0, concat_axis=0, tiled=True)  28.1 us
    reduce_sum x1, other arithmetic, green_points(): return jnp.stack([jnp.sum(real, axis=0), jnp.sum(imag, axis=0)])  19.3 us
    psum x1, blocking collectives, shards(): velocity = lax.psum(jnp.sum(got, axis=0), 'point')  13.9 us
    all_to_all x1, waiting for transfers between devices, shards(): lax.all_to_all(spread, 'panel', split_axis=0, concat_axis=0, tiled=True)  12.5 us
    all_to_all x1, starting transfers between devices, shards(): lax.all_to_all(spread, 'panel', split_axis=0, concat_axis=0, tiled=True)  4.62 us
  transfers between devices with their start and end apart: 1, of which 1 were waited for; matrix products, arithmetic and copies ran while one was open for 0% of the time, Pallas kernels for 0%

profile of v1, /device:TPU:1, one launch (start us, length us, event | category | flops | bytes accessed | tf_op | source)
XLA Modules:
  0.0 81.6 jit_solution(7250340246742215430)
XLA Ops:
  0.0 0.0 copy-start.3
  0.0 0.0 copy-start.4
  0.0 0.8 fusion.7
  0.8 0.0 copy-done.3
  0.8 0.0 copy-done.4
  0.8 0.0 copy-start.2
  0.8 0.0 copy-start
  0.8 0.9 %convolution_bitcast_fusion = f32[64,2,128]{2,0,1:T(8,128)S(1)} fusion(s32[2048]{0:T(1024)S(1)} %copy-done.4, f32[64,2048]{1,0:T(8,128)S(1)} %fusion.7, f32[2,2048]{1,0:T(2,128)S(1)} %copy-done.3), kind=kOutput, calls=%fused_computation.7 | convolution fusion | flops 403177472 | bytes 614400 | tf_op jit(solution)/shard_map/dot_general | solution.py:37
  1.7 0.1 copy.8
  1.7 0.0 copy-start.1
  1.7 28.1 %all_to_all.10 = f32[64,2,128]{2,1,0:T(2,128)S(1)} all-to-all(f32[64,2,128]{2,1,0:T(2,128)S(1)} %copy.8), channel_id=1, replica_groups=mesh['panel'=64,'point'=8] {'panel'}, dimensions={0} | all-to-all | bytes 131072 | tf_op jit(solution)/shard_map/all_to_all | solution.py:41
  29.8 0.1 reduce_sum.27
  29.9 13.9 %psum.7 = f32[2,128]{1,0:T(2,128)S(1)} all-reduce(f32[2,128]{1,0:T(2,128)S(1)} %reduce_sum.27), channel_id=1, replica_groups=mesh['panel'=64,'point'=8] {'point'}, use_global_device_ids=true, to_apply=%region_1.0 | all-reduce | flops 256 | bytes 2048 | tf_op jit(solution)/shard_map/psum | solution.py:42
  43.7 0.0 copy-done.2
  43.8 0.0 copy-done
  43.8 0.7 broadcast_in_dim.2
  44.5 4.6 %all-to-all-start.1 = ((f32[64,5,128]{2,1,0:T(8,128)}), f32[64,5,128]{2,1,0:T(8,128)S(1)}, u32[]{:S(2)}, u32[]{:S(2)}) async-start(f32[64,5,128]{2,1,0:T(8,128)} %broadcast_in_dim.2), calls=%async_computation.1 | async-start | bytes 524288 | tf_op jit(solution)/shard_map/all_to_all | solution.py:46
  49.1 0.0 copy-done.1
  49.1 12.5 %all-to-all-done.1 = f32[64,5,128]{2,1,0:T(8,128)S(1)} async-done(((f32[64,5,128]{2,1,0:T(8,128)}), f32[64,5,128]{2,1,0:T(8,128)S(1)}, u32[]{:S(2)}, u32[]{:S(2)}) %all-to-all-start.1) | async-done | bytes 163872 | tf_op jit(solution)/shard_map/all_to_all | solution.py:46
  61.6 0.1 fusion.10
  61.8 19.3 %subtract_reduce_fusion = (f32[128]{0:T(128)S(1)}, f32[128]{0:T(128)S(1)}) fusion(f32[8192]{0:T(1024)S(1)} %bitcast.34, f32[8192]{0:T(1024)S(1)} %bitcast.35, f32[128]{0:T(128)S(1)} %get-tuple-element.13, f32[8192]{0:T(1024)S(1)} %bitcast.36, f32[128]{0:T(128)S(1)} %get-tuple-element.14, f32[8192]{0:T(1024)S(1)} %bitcast.37, f32[128]{0:T(128)S(1)} %get-tuple-element.12, ...), kind=kLoop, calls=%fused_computation.1 | loop fusion | flops 22019840 | bytes 166400 | tf_op jit(solution)/shard_map/reduce_sum | solution.py:23
  81.0 0.6 pad_maximum_fusion.1
  (3 shorter events, 0.0 us)
Async XLA Ops:
  0.0 0.8 copy-start.3
  0.0 0.8 copy-start.4
  0.8 43.0 %copy-start.2 = (f32[128]{0:T(128)S(1)}, f32[128]{0:T(128)}, u32[]{:S(2)}) copy-start(f32[128]{0:T(128)} %param.10) | copy-start | bytes 1540
  0.8 43.0 %copy-start = (f32[3,128]{1,0:T(4,128)S(1)}, f32[3,128]{1,0:T(4,128)}, u32[]{:S(2)}) copy-start(f32[3,128]{1,0:T(4,128)} %param.9) | copy-start | bytes 4612
  1.7 47.4 %copy-start.1 = (f32[3,128]{1,0:T(4,128)S(1)}, f32[3,128]{1,0:T(4,128)}, u32[]{:S(2)}) copy-start(f32[3,128]{1,0:T(4,128)} %param.11) | copy-start | bytes 4612
  44.5 17.1 %all-to-all-start.1 = ((f32[64,5,128]{2,1,0:T(8,128)}), f32[64,5,128]{2,1,0:T(8,128)S(1)}, u32[]{:S(2)}, u32[]{:S(2)}) async-start(f32[64,5,128]{2,1,0:T(8,128)} %broadcast_in_dim.2), calls=%async_computation.1 | async-start | bytes 524288 | tf_op jit(solution)/shard_map/all_to_all | solution.py:46

commit v2 on v1

--- a/solution.py
+++ b/solution.py
@@ -37,13 +37,19 @@
     partial = jnp.dot(
         weighted, panel_hot, precision=lax.Precision.HIGHEST, preferred_element_type=jnp.float32
     )
-    partial = partial.reshape(2, slab_count, slab_width).transpose(1, 0, 2)
-    got = lax.all_to_all(partial, "panel", split_axis=0, concat_axis=0, tiled=True)
-    velocity = lax.psum(jnp.sum(got, axis=0), "point")
-    strength = jnp.stack([-panel_area * velocity[1], panel_area * velocity[0]])
-    packed = jnp.concatenate([strength, panel_centroid], axis=0)
-    spread = jnp.broadcast_to(packed[None], (slab_count,) + packed.shape)
-    gathered = lax.all_to_all(spread, "panel", split_axis=0, concat_axis=0, tiled=True)
+    group = ("panel", "point")
+    device_count = slab_count * lax.axis_size("point")
+    share = slab_count * slab_width // device_count
+    partial = partial.reshape(2, device_count, share).transpose(1, 0, 2)
+    got = lax.all_to_all(partial, group, split_axis=0, concat_axis=0, tiled=True)
+    velocity = jnp.sum(got, axis=0)
+    start = lax.axis_index("point") * share
+    area = lax.dynamic_slice_in_dim(panel_area, start, share)
+    centroid = lax.dynamic_slice_in_dim(panel_centroid, start, share, axis=1)
+    strength = jnp.stack([-area * velocity[1], area * velocity[0]])
+    packed = jnp.concatenate([strength, centroid], axis=0)
+    spread = jnp.broadcast_to(packed[None], (device_count,) + packed.shape)
+    gathered = lax.all_to_all(spread, group, split_axis=0, concat_axis=0, tiled=True)
     every = gathered.transpose(1, 0, 2).reshape(packed.shape[0], -1)
     return green_points(every[2:5], every[0:2], field_points)
 

time: 82.7 us -> 138 us (1.67)
  waiting for transfers between devices: 12.5 us -> 75.6 us
  blocking collectives: 41.9 us -> 0 us
  starting transfers between devices: 4.62 us -> 30.8 us
  local copies, waits for them, and re-layouts: 0.91 us -> 7.54 us
  other arithmetic: 20.7 us -> 22.1 us
    all_to_all x1 -> x2, waiting for transfers between devices: 12.5 us -> 75.6 us  [the longest x1 53.4 us: shards(): lax.all_to_all(spread, group, split_axis=0, concat_axis=0, tiled=True)]
    all_to_all x1 -> x0, blocking collectives: 28.1 us -> none  [shards(): lax.all_to_all(partial, 'panel', split_axis=0, concat_axis=0, tiled=True)]
    all_to_all x1 -> x2, starting transfers between devices: 4.62 us -> 30.8 us  [the longest x1 22.1 us: shards(): lax.all_to_all(partial, group, split_axis=0, concat_axis=0, tiled=True)]
    psum x1 -> x0, blocking collectives: 13.9 us -> none  [shards(): velocity = lax.psum(jnp.sum(got, axis=0), 'point')]
    slice x1, local copies, waits for them, and re-layouts: 0.12 us -> 3.95 us  [green_points(): real = strength[0][:, None] * cosine_part - strength[1][:, None] * sine_part]
  transfers between devices with their start and end apart: 1 -> 2, of which waited for: 1 -> 2; matrix products, arithmetic and copies ran while one was open for 0% -> 0% of each run, Pallas kernels for 0% -> 0%
where the time goes in v2:
time: 138 us; the launch traced here: 137 us
  waiting for transfers between devices  75.6 us (55%)
  starting transfers between devices  30.8 us (22%)
  other arithmetic  22.1 us (16%)
  local copies, waits for them, and re-layouts  7.54 us (5%)
    all_to_all x1, waiting for transfers between devices, shards(): lax.all_to_all(spread, group, split_axis=0, concat_axis=0, tiled=True)  53.4 us
    all_to_all x1, waiting for transfers between devices, shards(): lax.all_to_all(partial, group, split_axis=0, concat_axis=0, tiled=True)  22.3 us
    all_to_all x1, starting transfers between devices, shards(): lax.all_to_all(partial, group, split_axis=0, concat_axis=0, tiled=True)  22.1 us
    reduce_sum x1, other arithmetic, green_points(): return jnp.stack([jnp.sum(real, axis=0), jnp.sum(imag, axis=0)])  19.3 us
    all_to_all x1, starting transfers between devices, shards(): lax.all_to_all(spread, group, split_axis=0, concat_axis=0, tiled=True)  8.68 us
    slice x1, local copies, waits for them, and re-layouts, green_points(): real = strength[0][:, None] * cosine_part - strength[1][:, None] * sine_part  3.95 us
  transfers between devices with their start and end apart: 2, of which 2 were waited for; matrix products, arithmetic and copies ran while one was open for 0% of the time, Pallas kernels for 0%

profile of v2, /device:TPU:1, one launch (start us, length us, event | category | flops | bytes accessed | tf_op | source)
XLA Modules:
  0.0 137.0 jit_solution(9606343529736760064)
XLA Ops:
  0.0 0.0 copy-start
  0.0 0.0 copy-start.1
  0.0 0.8 fusion.3
  0.8 0.8 broadcast_multiply_fusion
  1.6 0.0 copy-done.1
  1.6 0.0 copy-start.3
  1.6 0.8 fusion.1
  2.5 0.2 reshape.53
  2.6 1.2 copy.8
  3.8 22.1 %all-to-all-start = ((f32[512,2,16]{2,1,0:T(2,128)}), f32[512,2,16]{2,1,0:T(2,128)S(1)}, u32[]{:S(2)}, u32[]{:S(2)}) async-start(f32[512,2,16]{2,1,0:T(2,128)} %copy.8), calls=%async_computation | async-start | bytes 1048576 | tf_op jit(solution)/shard_map/all_to_all | solution.py:44
  26.0 0.0 copy-done
  26.0 0.1 constant_dynamic-slice_fusion
  26.1 22.3 %all-to-all-done = f32[512,2,16]{2,1,0:T(2,128)S(1)} async-done(((f32[512,2,16]{2,1,0:T(2,128)}), f32[512,2,16]{2,1,0:T(2,128)S(1)}, u32[]{:S(2)}, u32[]{:S(2)}) %all-to-all-start) | async-done | bytes 65568 | tf_op jit(solution)/shard_map/all_to_all | solution.py:44
  48.3 0.5 reduce_sum.27
  48.9 0.0 copy-done.3
  48.9 0.1 fusion.5
  49.0 1.5 %broadcast_in_dim.2 = f32[512,5,16]{2,1,0:T(8,128)} broadcast(f32[5,16]{1,0:T(8,128)S(1)} %pad_maximum_fusion), dimensions={1,2} | broadcast | bytes 164160 | tf_op jit(solution)/shard_map/broadcast_in_dim | solution.py:51
  50.5 0.0 copy-start.2
  50.5 8.7 %all-to-all-start.1 = ((f32[512,5,16]{2,1,0:T(8,128)}), f32[512,5,16]{2,1,0:T(8,128)S(1)}, u32[]{:S(2)}, u32[]{:S(2)}) async-start(f32[512,5,16]{2,1,0:T(8,128)} %broadcast_in_dim.2), calls=%async_computation.1 | async-start | bytes 4194304 | tf_op jit(solution)/shard_map/all_to_all | solution.py:52
  59.2 0.0 copy-done.2
  59.2 53.4 %all-to-all-done.1 = f32[512,5,16]{2,1,0:T(8,128)S(1)} async-done(((f32[512,5,16]{2,1,0:T(8,128)}), f32[512,5,16]{2,1,0:T(8,128)S(1)}, u32[]{:S(2)}, u32[]{:S(2)}) %all-to-all-start.1) | async-done | bytes 163872 | tf_op jit(solution)/shard_map/all_to_all | solution.py:52
  112.6 4.0 %slice_reduce_fusion.4 = (f32[512,16]{1,0:T(8,128)S(1)}, f32[512,16]{1,0:T(8,128)S(1)}, f32[512,16]{1,0:T(8,128)S(1)}, f32[512,16]{1,0:T(8,128)S(1)}, f32[512,16]{1,0:T(8,128)S(1)}) fusion(f32[5,512,16]{2,0,1:T(8,128)S(1)} %bitcast.25), kind=kLoop, calls=%fused_computation.17 | loop fusion | bytes 327680 | tf_op jit(solution)/shard_map/slice | solution.py:21
  116.5 0.1 mul.103
  116.6 0.1 mul.92
  116.8 0.1 sub.56
  116.9 0.1 sub.61
  117.0 0.1 sub.66
  117.2 19.3 %subtract_reduce_fusion = (f32[128]{0:T(128)S(1)}, f32[128]{0:T(128)S(1)}) fusion(f32[8192]{0:T(1024)S(1)} %mul.103, f32[8192]{0:T(1024)S(1)} %sub.66, f32[128]{0:T(128)S(1)} %get-tuple-element.13, f32[8192]{0:T(1024)S(1)} %sub.61, f32[128]{0:T(128)S(1)} %get-tuple-element.14, f32[8192]{0:T(1024)S(1)} %sub.56, f32[128]{0:T(128)S(1)} %get-tuple-element.12, ...), kind=kLoop, calls=%fused_computation.1 | loop fusion | flops 22019840 | bytes 166400 | tf_op jit(solution)/shard_map/reduce_sum | solution.py:23
  136.5 0.6 pad_maximum_fusion.1
  (2 shorter events, 0.0 us)
Async XLA Ops:
  0.0 26.0 %copy-start = (f32[3,128]{1,0:T(4,128)S(1)}, f32[3,128]{1,0:T(4,128)}, u32[]{:S(2)}) copy-start(f32[3,128]{1,0:T(4,128)} %param.9) | copy-start | bytes 4612
  0.0 1.6 %copy-start.1 = (s32[2048]{0:T(1024)S(1)}, s32[2048]{0:T(1024)}, u32[]{:S(2)}) copy-start(s32[2048]{0:T(1024)} %param.8) | copy-start | bytes 24580
  1.6 47.3 %copy-start.3 = (f32[128]{0:T(128)S(1)}, f32[128]{0:T(128)}, u32[]{:S(2)}) copy-start(f32[128]{0:T(128)} %param.10) | copy-start | bytes 1540
  3.8 44.5 %all-to-all-start = ((f32[512,2,16]{2,1,0:T(2,128)}), f32[512,2,16]{2,1,0:T(2,128)S(1)}, u32[]{:S(2)}, u32[]{:S(2)}) async-start(f32[512,2,16]{2,1,0:T(2,128)} %copy.8), calls=%async_computation | async-start | bytes 1048576 | tf_op jit(solution)/shard_map/all_to_all | solution.py:44
  50.5 8.7 %copy-start.2 = (f32[3,128]{1,0:T(4,128)S(1)}, f32[3,128]{1,0:T(4,128)}, u32[]{:S(2)}) copy-start(f32[3,128]{1,0:T(4,128)} %param.11) | copy-start | bytes 4612
  50.5 62.1 %all-to-all-start.1 = ((f32[512,5,16]{2,1,0:T(8,128)}), f32[512,5,16]{2,1,0:T(8,128)S(1)}, u32[]{:S(2)}, u32[]{:S(2)}) async-start(f32[512,5,16]{2,1,0:T(8,128)} %broadcast_in_dim.2), calls=%async_computation.1 | async-start | bytes 4194304 | tf_op jit(solution)/shard_map/all_to_all | solution.py:52

commit v3 on v1

--- a/solution.py
+++ b/solution.py
@@ -9,15 +9,17 @@
 FOUR_PI = 4.0 * math.pi
 
 
-def green_points(centers, strength, points):
+def kernel_parts(centers, points):
     delta_x = points[0][None, :] - centers[0][:, None]
     delta_y = points[1][None, :] - centers[1][:, None]
     delta_z = points[2][None, :] - centers[2][:, None]
     distance = jnp.sqrt(delta_x * delta_x + delta_y * delta_y + delta_z * delta_z)
     inverse = 1.0 / (FOUR_PI * distance)
     phase_angle = WAVENUMBER * distance
-    cosine_part = jnp.cos(phase_angle) * inverse
-    sine_part = jnp.sin(phase_angle) * inverse
+    return jnp.cos(phase_angle) * inverse, jnp.sin(phase_angle) * inverse
+
+
+def contract(strength, cosine_part, sine_part):
     real = strength[0][:, None] * cosine_part - strength[1][:, None] * sine_part
     imag = strength[0][:, None] * sine_part + strength[1][:, None] * cosine_part
     return jnp.stack([jnp.sum(real, axis=0), jnp.sum(imag, axis=0)])
@@ -38,14 +40,17 @@
         weighted, panel_hot, precision=lax.Precision.HIGHEST, preferred_element_type=jnp.float32
     )
     partial = partial.reshape(2, slab_count, slab_width).transpose(1, 0, 2)
-    got = lax.all_to_all(partial, "panel", split_axis=0, concat_axis=0, tiled=True)
-    velocity = lax.psum(jnp.sum(got, axis=0), "point")
+    centroid_copies = jnp.broadcast_to(panel_centroid[None], (slab_count,) + panel_centroid.shape)
+    outgoing = jnp.concatenate([partial, centroid_copies], axis=1)
+    got = lax.all_to_all(outgoing, "panel", split_axis=0, concat_axis=0, tiled=True)
+    velocity = lax.psum(jnp.sum(got[:, 0:2], axis=0), "point")
+    centers = got[:, 2:5].transpose(1, 0, 2).reshape(3, -1)
+    cosine_part, sine_part = lax.optimization_barrier(kernel_parts(centers, field_points))
     strength = jnp.stack([-panel_area * velocity[1], panel_area * velocity[0]])
-    packed = jnp.concatenate([strength, panel_centroid], axis=0)
-    spread = jnp.broadcast_to(packed[None], (slab_count,) + packed.shape)
+    spread = jnp.broadcast_to(strength[None], (slab_count,) + strength.shape)
     gathered = lax.all_to_all(spread, "panel", split_axis=0, concat_axis=0, tiled=True)
-    every = gathered.transpose(1, 0, 2).reshape(packed.shape[0], -1)
-    return green_points(every[2:5], every[0:2], field_points)
+    every = gathered.transpose(1, 0, 2).reshape(2, -1)
+    return contract(every, cosine_part, sine_part)
 
 
 def solution(mesh):

time: 82.7 us -> 83.3 us (level)
  blocking collectives: 41.9 us -> 14.8 us
  starting transfers between devices: 4.62 us -> 21.7 us
  other arithmetic: 20.7 us -> 29.9 us
  local copies, waits for them, and re-layouts: 0.91 us -> 2.36 us
    all_to_all x1 -> x0, blocking collectives: 28.1 us -> none  [shards(): lax.all_to_all(partial, 'panel', split_axis=0, concat_axis=0, tiled=True)]
    mul x0 -> x1, other arithmetic: none -> 20.1 us  [kernel_parts(): return (jnp.cos(phase_angle) * inverse, jnp.sin(phase_angle) * inverse)]
    all_to_all x0 -> x1, starting transfers between devices: none -> 17.1 us  [shards(): lax.all_to_all(outgoing, 'panel', split_axis=0, concat_axis=0, tiled=True)]
    all_to_all x1, waiting for transfers between devices: 12.5 us -> 0.01 us  [shards(): lax.all_to_all(spread, 'panel', split_axis=0, concat_axis=0, tiled=True)]
    reduce_sum x2, other arithmetic: 19.4 us -> 7.08 us  [the longest x1 7.01 us: contract(): return jnp.stack([jnp.sum(real, axis=0), jnp.sum(imag, axis=0)])]
    all_to_all x0 -> x1, waiting for transfers between devices: none -> 12 us  [shards(): lax.all_to_all(outgoing, 'panel', split_axis=0, concat_axis=0, tiled=True)]
    psum x1, blocking collectives: 13.9 us -> 14.8 us  [shards(): velocity = lax.psum(jnp.sum(got[:, 0:2], axis=0), 'point')]
  transfers between devices with their start and end apart: 1 -> 2, of which waited for: 1 -> 1; matrix products, arithmetic and copies ran while one was open for 0% -> 25% of each run, Pallas kernels for 0% -> 0%
where the time goes in v3:
time: 83.3 us; the launch traced here: 82.4 us
  other arithmetic  29.9 us (36%)
  starting transfers between devices  21.7 us (26%)
  blocking collectives  14.8 us (18%)
  waiting for transfers between devices  12 us (14%)
  local copies, waits for them, and re-layouts  2.36 us (3%)
  matrix products  1.57 us (2%)
    mul x1, other arithmetic, kernel_parts(): return (jnp.cos(phase_angle) * inverse, jnp.sin(phase_angle) * inverse)  20.1 us
    all_to_all x1, starting transfers between devices, shards(): lax.all_to_all(outgoing, 'panel', split_axis=0, concat_axis=0, tiled=True)  17.1 us
    psum x1, blocking collectives, shards(): velocity = lax.psum(jnp.sum(got[:, 0:2], axis=0), 'point')  14.8 us
    all_to_all x1, waiting for transfers between devices, shards(): lax.all_to_all(outgoing, 'panel', split_axis=0, concat_axis=0, tiled=True)  12 us
    reduce_sum x1, other arithmetic, contract(): return jnp.stack([jnp.sum(real, axis=0), jnp.sum(imag, axis=0)])  7.01 us
    all_to_all x1, starting transfers between devices, shards(): lax.all_to_all(spread, 'panel', split_axis=0, concat_axis=0, tiled=True)  4.54 us
  transfers between devices with their start and end apart: 2, of which 1 were waited for; matrix products, arithmetic and copies ran while one was open for 25% of the time, Pallas kernels for 0%

profile of v3, /device:TPU:1, one launch (start us, length us, event | category | flops | bytes accessed | tf_op | source)
XLA Modules:
  0.0 82.4 jit_solution(9306345595922590570)
XLA Ops:
  0.0 0.7 fusion.7
  0.7 1.6 %convolution_bitcast_fusion = f32[64,2,128]{2,0,1:T(8,128)S(1)} fusion(s32[2048]{0:T(1024)} %param.8, f32[64,2048]{1,0:T(8,128)S(1)} %fusion.7, f32[2,2048]{1,0:T(2,128)} %param.6), kind=kOutput, calls=%fused_computation.7 | convolution fusion | flops 403177472 | bytes 614400 | tf_op jit(solution)/shard_map/dot_general | solution.py:39
  2.3 0.1 copy.8
  2.4 0.7 broadcast_in_dim.4
  3.1 0.7 pad_maximum_fusion
  3.8 17.1 %all-to-all-start = ((f32[64,5,128]{2,1,0:T(8,128)}), f32[64,5,128]{2,1,0:T(8,128)S(1)}, u32[]{:S(2)}, u32[]{:S(2)}) async-start(f32[64,5,128]{2,1,0:T(8,128)} %pad_maximum_fusion), calls=%async_computation | async-start | bytes 524288 | tf_op jit(solution)/shard_map/all_to_all | solution.py:45
  21.0 0.8 slice_bitcast_fusion.3
  21.8 12.0 %all-to-all-done = f32[64,5,128]{2,1,0:T(8,128)S(1)} async-done(((f32[64,5,128]{2,1,0:T(8,128)}), f32[64,5,128]{2,1,0:T(8,128)S(1)}, u32[]{:S(2)}, u32[]{:S(2)}) %all-to-all-start) | async-done | bytes 163872 | tf_op jit(solution)/shard_map/all_to_all | solution.py:45
  33.8 0.1 fusion.10
  33.9 0.1 slice_reduce_fusion
  34.0 14.8 %psum.7 = f32[2,128]{1,0:T(2,128)S(1)} all-reduce(f32[2,128]{1,0:T(2,128)S(1)} %slice_reduce_fusion), channel_id=1, replica_groups=mesh['panel'=64,'point'=8] {'point'}, use_global_device_ids=true, to_apply=%region_1.0 | all-reduce | flops 256 | bytes 2048 | tf_op jit(solution)/shard_map/psum | solution.py:46
  48.8 0.7 fusion.9
  49.5 0.7 broadcast_in_dim.5
  50.1 4.5 %all-to-all-start.1 = ((f32[64,2,128]{2,1,0:T(2,128)}), f32[64,2,128]{2,1,0:T(2,128)S(1)}, u32[]{:S(2)}, u32[]{:S(2)}) async-start(f32[64,2,128]{2,1,0:T(2,128)} %broadcast_in_dim.5), calls=%async_computation.1 | async-start | bytes 131072 | tf_op jit(solution)/shard_map/all_to_all | solution.py:51
  54.7 20.1 %sine_multiply_fusion = (f32[8192,128]{1,0:T(8,128)}, f32[8192,128]{1,0:T(8,128)}) fusion(f32[8192]{0:T(1024)S(1)} %bitcast.36, f32[128]{0:T(128)S(1)} %get-tuple-element.19, f32[8192]{0:T(1024)S(1)} %bitcast.37, f32[128]{0:T(128)S(1)} %get-tuple-element.20, f32[8192]{0:T(1024)S(1)} %bitcast.35, f32[128]{0:T(128)S(1)} %get-tuple-element.18), kind=kLoop, calls=%fused_computation.2 | loop fusion | flops 13631488 | bytes 8488448 | tf_op jit(solution)/shard_map/mul | solution.py:19
  74.8 0.0 all-to-all-done.1
  74.8 0.1 fusion.11
  74.8 7.0 %subtract_reduce_fusion = (f32[128]{0:T(128)S(1)}, f32[128]{0:T(128)S(1)}) fusion(f32[8192,128]{1,0:T(8,128)} %get-tuple-element.8, f32[8192,128]{1,0:T(8,128)} %get-tuple-element.7, f32[8192]{0:T(1024)S(1)} %bitcast.39, f32[8192]{0:T(1024)S(1)} %bitcast.38), kind=kLoop, calls=%fused_computation.1 | loop fusion | flops 8388352 | bytes 8455168 | tf_op jit(solution)/shard_map/reduce_sum | solution.py:25
  81.8 0.6 pad_maximum_fusion.2
  (2 shorter events, 0.0 us)
Async XLA Ops:
  3.8 30.0 %all-to-all-start = ((f32[64,5,128]{2,1,0:T(8,128)}), f32[64,5,128]{2,1,0:T(8,128)S(1)}, u32[]{:S(2)}, u32[]{:S(2)}) async-start(f32[64,5,128]{2,1,0:T(8,128)} %pad_maximum_fusion), calls=%async_computation | async-start | bytes 524288 | tf_op jit(solution)/shard_map/all_to_all | solution.py:45
  50.1 24.6 %all-to-all-start.1 = ((f32[64,2,128]{2,1,0:T(2,128)}), f32[64,2,128]{2,1,0:T(2,128)S(1)}, u32[]{:S(2)}, u32[]{:S(2)}) async-start(f32[64,2,128]{2,1,0:T(2,128)} %broadcast_in_dim.5), calls=%async_computation.1 | async-start | bytes 131072 | tf_op jit(solution)/shard_map/all_to_all | solution.py:51

commit v4 on v1

--- a/solution.py
+++ b/solution.py
@@ -39,7 +39,10 @@
     )
     partial = partial.reshape(2, slab_count, slab_width).transpose(1, 0, 2)
     got = lax.all_to_all(partial, "panel", split_axis=0, concat_axis=0, tiled=True)
-    velocity = lax.psum(jnp.sum(got, axis=0), "point")
+    column = jnp.sum(got, axis=0)
+    point_count = lax.axis_size("point")
+    copies = jnp.broadcast_to(column[None], (point_count,) + column.shape)
+    velocity = jnp.sum(lax.all_to_all(copies, "point", split_axis=0, concat_axis=0, tiled=True), axis=0)
     strength = jnp.stack([-panel_area * velocity[1], panel_area * velocity[0]])
     packed = jnp.concatenate([strength, panel_centroid], axis=0)
     spread = jnp.broadcast_to(packed[None], (slab_count,) + packed.shape)

time: 82.7 us -> 80 us (0.967)
  blocking collectives: 41.9 us -> 38.9 us
    psum x1 -> x0, blocking collectives: 13.9 us -> none  [shards(): velocity = lax.psum(jnp.sum(got, axis=0), 'point')]
    all_to_all x0 -> x1, blocking collectives: none -> 10.8 us  [shards(): lax.all_to_all(copies, 'point', split_axis=0, concat_axis=0, tiled=True)]
where the time goes in v4:
time: 80 us; the launch traced here: 79.1 us
  blocking collectives  38.9 us (49%)
  other arithmetic  20.7 us (26%)
  waiting for transfers between devices  13 us (16%)
  starting transfers between devices  4.62 us (6%)
  local copies, waits for them, and re-layouts  0.92 us (1%)
  matrix products  0.86 us (1%)
    all_to_all x1, blocking collectives, shards(): lax.all_to_all(partial, 'panel', split_axis=0, concat_axis=0, tiled=True)  28.1 us
    reduce_sum x1, other arithmetic, green_points(): return jnp.stack([jnp.sum(real, axis=0), jnp.sum(imag, axis=0)])  19.3 us
    all_to_all x1, waiting for transfers between devices, shards(): lax.all_to_all(spread, 'panel', split_axis=0, concat_axis=0, tiled=True)  13 us
    all_to_all x1, blocking collectives, shards(): lax.all_to_all(copies, 'point', split_axis=0, concat_axis=0, tiled=True)  10.8 us
    all_to_all x1, starting transfers between devices, shards(): lax.all_to_all(spread, 'panel', split_axis=0, concat_axis=0, tiled=True)  4.62 us
  transfers between devices with their start and end apart: 1, of which 1 were waited for; matrix products, arithmetic and copies ran while one was open for 0% of the time, Pallas kernels for 0%

profile of v4, /device:TPU:1, one launch (start us, length us, event | category | flops | bytes accessed | tf_op | source)
XLA Modules:
  0.0 79.1 jit_solution(18057623016647084587)
XLA Ops:
  0.0 0.0 copy-start.3
  0.0 0.0 copy-start.4
  0.0 0.8 fusion.7
  0.8 0.0 copy-done.3
  0.8 0.0 copy-done.4
  0.8 0.0 copy-start.2
  0.8 0.0 copy-start
  0.8 0.9 %convolution_bitcast_fusion = f32[64,2,128]{2,0,1:T(8,128)S(1)} fusion(s32[2048]{0:T(1024)S(1)} %copy-done.4, f32[64,2048]{1,0:T(8,128)S(1)} %fusion.7, f32[2,2048]{1,0:T(2,128)S(1)} %copy-done.3), kind=kOutput, calls=%fused_computation.7 | convolution fusion | flops 403177472 | bytes 614400 | tf_op jit(solution)/shard_map/dot_general | solution.py:37
  1.7 0.1 copy.9
  1.7 0.0 copy-start.1
  1.7 28.1 %all_to_all.15 = f32[64,2,128]{2,1,0:T(2,128)S(1)} all-to-all(f32[64,2,128]{2,1,0:T(2,128)S(1)} %copy.9), channel_id=1, replica_groups=mesh['panel'=64,'point'=8] {'panel'}, dimensions={0} | all-to-all | bytes 131072 | tf_op jit(solution)/shard_map/all_to_all | solution.py:41
  29.8 0.1 reduce_sum.36
  29.9 10.8 %all_to_all.16 = f32[8,2,128]{2,1,0:T(2,128)S(1)} all-to-all(f32[8,2,128]{2,1,0:T(2,128)S(1)} %broadcast_in_dim.4), channel_id=1, replica_groups=mesh['panel'=64,'point'=8] {'point'}, dimensions={0} | all-to-all | bytes 16384 | tf_op jit(solution)/shard_map/all_to_all | solution.py:45
  40.7 0.0 copy-done.2
  40.7 0.0 copy-done
  40.8 0.7 broadcast_in_dim.5
  41.5 4.6 %all-to-all-start.2 = ((f32[64,5,128]{2,1,0:T(8,128)}), f32[64,5,128]{2,1,0:T(8,128)S(1)}, u32[]{:S(2)}, u32[]{:S(2)}) async-start(f32[64,5,128]{2,1,0:T(8,128)} %broadcast_in_dim.5), calls=%async_computation.2 | async-start | bytes 524288 | tf_op jit(solution)/shard_map/all_to_all | solution.py:49
  46.1 0.0 copy-done.1
  46.1 13.0 %all-to-all-done.2 = f32[64,5,128]{2,1,0:T(8,128)S(1)} async-done(((f32[64,5,128]{2,1,0:T(8,128)}), f32[64,5,128]{2,1,0:T(8,128)S(1)}, u32[]{:S(2)}, u32[]{:S(2)}) %all-to-all-start.2) | async-done | bytes 163872 | tf_op jit(solution)/shard_map/all_to_all | solution.py:49
  59.1 0.1 fusion.10
  59.2 19.3 %subtract_reduce_fusion = (f32[128]{0:T(128)S(1)}, f32[128]{0:T(128)S(1)}) fusion(f32[8192]{0:T(1024)S(1)} %bitcast.34, f32[8192]{0:T(1024)S(1)} %bitcast.35, f32[128]{0:T(128)S(1)} %get-tuple-element.13, f32[8192]{0:T(1024)S(1)} %bitcast.36, f32[128]{0:T(128)S(1)} %get-tuple-element.14, f32[8192]{0:T(1024)S(1)} %bitcast.37, f32[128]{0:T(128)S(1)} %get-tuple-element.12, ...), kind=kLoop, calls=%fused_computation.1 | loop fusion | flops 22019840 | bytes 166400 | tf_op jit(solution)/shard_map/reduce_sum | solution.py:23
  78.5 0.6 pad_maximum_fusion.1
  (5 shorter events, 0.0 us)
Async XLA Ops:
  0.0 0.8 copy-start.3
  0.0 0.8 copy-start.4
  0.8 39.9 %copy-start.2 = (f32[128]{0:T(128)S(1)}, f32[128]{0:T(128)}, u32[]{:S(2)}) copy-start(f32[128]{0:T(128)} %param.10) | copy-start | bytes 1540
  0.8 39.9 %copy-start = (f32[3,128]{1,0:T(4,128)S(1)}, f32[3,128]{1,0:T(4,128)}, u32[]{:S(2)}) copy-start(f32[3,128]{1,0:T(4,128)} %param.9) | copy-start | bytes 4612
  1.7 44.4 %copy-start.1 = (f32[3,128]{1,0:T(4,128)S(1)}, f32[3,128]{1,0:T(4,128)}, u32[]{:S(2)}) copy-start(f32[3,128]{1,0:T(4,128)} %param.11) | copy-start | bytes 4612
  41.5 17.6 %all-to-all-start.2 = ((f32[64,5,128]{2,1,0:T(8,128)}), f32[64,5,128]{2,1,0:T(8,128)S(1)}, u32[]{:S(2)}, u32[]{:S(2)}) async-start(f32[64,5,128]{2,1,0:T(8,128)} %broadcast_in_dim.5), calls=%async_computation.2 | async-start | bytes 524288 | tf_op jit(solution)/shard_map/all_to_all | solution.py:49

commit v5 on v4

--- a/solution.py
+++ b/solution.py
@@ -3,24 +3,88 @@
 import jax
 import jax.numpy as jnp
 from jax import lax
+from jax.experimental import pallas as pl
+from jax.experimental.pallas import tpu as pltpu
 from jax.sharding import PartitionSpec as P
 
 WAVENUMBER = 40.0
 FOUR_PI = 4.0 * math.pi
 
 
-def green_points(centers, strength, points):
-    delta_x = points[0][None, :] - centers[0][:, None]
-    delta_y = points[1][None, :] - centers[1][:, None]
-    delta_z = points[2][None, :] - centers[2][:, None]
-    distance = jnp.sqrt(delta_x * delta_x + delta_y * delta_y + delta_z * delta_z)
-    inverse = 1.0 / (FOUR_PI * distance)
-    phase_angle = WAVENUMBER * distance
-    cosine_part = jnp.cos(phase_angle) * inverse
-    sine_part = jnp.sin(phase_angle) * inverse
-    real = strength[0][:, None] * cosine_part - strength[1][:, None] * sine_part
-    imag = strength[0][:, None] * sine_part + strength[1][:, None] * cosine_part
-    return jnp.stack([jnp.sum(real, axis=0), jnp.sum(imag, axis=0)])
+TWO_OVER_PI = 2.0 / math.pi
+HALF_PI_1 = 1.5703125
+HALF_PI_2 = 4.837512969970703125e-4
+HALF_PI_3 = 7.54978995489188216e-8
+GROUP = 16
+
+
+def sine_cosine(angle):
+    turns = jnp.floor(angle * TWO_OVER_PI + 0.5)
+    rest = ((angle - turns * HALF_PI_1) - turns * HALF_PI_2) - turns * HALF_PI_3
+    square = rest * rest
+    sine = rest + rest * square * (
+        -1.6666654611e-1 + square * (8.3321608736e-3 + square * -1.9515295891e-4)
+    )
+    cosine = 1.0 - 0.5 * square + square * square * (
+        4.166664568298827e-2 + square * (-1.388731625493765e-3 + square * 2.443315711809948e-5)
+    )
+    quadrant = turns.astype(jnp.int32)
+    swap = (quadrant & 1) == 1
+    sine_out = jnp.where(swap, cosine, sine)
+    cosine_out = jnp.where(swap, sine, cosine)
+    sine_out = jnp.where((quadrant & 2) == 2, -sine_out, sine_out)
+    cosine_out = jnp.where(((quadrant + 1) & 2) == 2, -cosine_out, cosine_out)
+    return sine_out, cosine_out
+
+
+def green_kernel(panel_ref, point_ref, out_ref, total_ref):
+    chunks = panel_ref.shape[0]
+    points = point_ref.shape[1]
+    for group in range(points // GROUP):
+        rows = pl.ds(group * GROUP, GROUP)
+        point_x = point_ref[0, rows, :]
+        point_y = point_ref[1, rows, :]
+        point_z = point_ref[2, rows, :]
+
+        def body(chunk, carry):
+            real_sum, imag_sum = carry
+            block = panel_ref[chunk]
+            shape = (GROUP, block.shape[1])
+            strength_re = jnp.broadcast_to(block[0:1], shape)
+            strength_im = jnp.broadcast_to(block[1:2], shape)
+            delta_x = point_x - jnp.broadcast_to(block[2:3], shape)
+            delta_y = point_y - jnp.broadcast_to(block[3:4], shape)
+            delta_z = point_z - jnp.broadcast_to(block[4:5], shape)
+            distance = jnp.sqrt(delta_x * delta_x + delta_y * delta_y + delta_z * delta_z)
+            inverse = 1.0 / (FOUR_PI * distance)
+            sine, cosine = sine_cosine(WAVENUMBER * distance)
+            cosine_part = cosine * inverse
+            sine_part = sine * inverse
+            real_sum = real_sum + (strength_re * cosine_part - strength_im * sine_part)
+            imag_sum = imag_sum + (strength_re * sine_part + strength_im * cosine_part)
+            return real_sum, imag_sum
+
+        zero = jnp.zeros((GROUP, panel_ref.shape[2]), jnp.float32)
+        real_sum, imag_sum = lax.fori_loop(0, chunks, body, (zero, zero), unroll=2)
+        total_ref[0, rows, :] = real_sum
+        total_ref[1, rows, :] = imag_sum
+    out_ref[0:1, :] = jnp.sum(total_ref[0].T, axis=0, keepdims=True)
+    out_ref[1:2, :] = jnp.sum(total_ref[1].T, axis=0, keepdims=True)
+
+
+def green(panels, field_points):
+    points = field_points.shape[1]
+    lanes = panels.shape[2]
+    spread = jnp.broadcast_to(field_points[:, :, None], (3, points, lanes))
+    pairs = panels.shape[0] * lanes * points
+    return pl.pallas_call(
+        green_kernel,
+        out_shape=jax.ShapeDtypeStruct((2, points), jnp.float32),
+        in_specs=[pl.BlockSpec(memory_space=pltpu.VMEM)] * 2,
+        out_specs=pl.BlockSpec(memory_space=pltpu.VMEM),
+        scratch_shapes=[pltpu.VMEM((2, points, lanes), jnp.float32)],
+        cost_estimate=pl.CostEstimate(flops=70 * pairs, transcendentals=2 * pairs, bytes_accessed=4 * (panels.size + spread.size + 2 * points)),
+    )(panels, spread)
 
 
 def shards(node_velocity, node_owner, node_panel, panel_centroid, panel_area, field_points):
@@ -47,8 +111,7 @@
     packed = jnp.concatenate([strength, panel_centroid], axis=0)
     spread = jnp.broadcast_to(packed[None], (slab_count,) + packed.shape)
     gathered = lax.all_to_all(spread, "panel", split_axis=0, concat_axis=0, tiled=True)
-    every = gathered.transpose(1, 0, 2).reshape(packed.shape[0], -1)
-    return green_points(every[2:5], every[0:2], field_points)
+    return green(gathered, field_points)
 
 
 def solution(mesh):

time: 80 us -> 74.8 us (0.935)
  other arithmetic: 20.7 us -> 0.87 us
  blocking collectives: 38.9 us -> 56.3 us
  Pallas kernels: 0 us -> 13.5 us
  waiting for transfers between devices: 13 us -> 0 us
  starting transfers between devices: 4.62 us -> 0 us
  local copies, waits for them, and re-layouts: 0.92 us -> 2.21 us
    reduce_sum x1 -> x0, other arithmetic: 19.3 us -> none  [green_points(): return jnp.stack([jnp.sum(real, axis=0), jnp.sum(imag, axis=0)])]
    all_to_all x0 -> x1, blocking collectives: none -> 17.5 us  [shards(): lax.all_to_all(spread, 'panel', split_axis=0, concat_axis=0, tiled=True)]
    pallas_call x0 -> x1, Pallas kernels: none -> 13.5 us  [green(): pl.pallas_call(green_kernel, out_shape=jax.ShapeDtypeStruct((2, points),...]
    all_to_all x1 -> x0, waiting for transfers between devices: 13 us -> none  [shards(): lax.all_to_all(spread, 'panel', split_axis=0, concat_axis=0, tiled=True)]
    all_to_all x1 -> x0, starting transfers between devices: 4.62 us -> none  [shards(): lax.all_to_all(spread, 'panel', split_axis=0, concat_axis=0, tiled=True)]
    unnamed x10, local copies, waits for them, and re-layouts: 0.03 us -> 1.33 us
  transfers between devices with their start and end apart: 1 -> 0, of which waited for: 1 -> 0; matrix products, arithmetic and copies ran while one was open for 0% -> 0% of each run, Pallas kernels for 0% -> 0%
where the time goes in v5:
time: 74.8 us; the launch traced here: 73.9 us
  blocking collectives  56.3 us (75%)
  Pallas kernels  13.5 us (18%)
  local copies, waits for them, and re-layouts  2.21 us (3%)
  other arithmetic  0.87 us (1%)
  matrix products  0.86 us (1%)
    all_to_all x1, blocking collectives, shards(): lax.all_to_all(partial, 'panel', split_axis=0, concat_axis=0, tiled=True)  28.1 us
    all_to_all x1, blocking collectives, shards(): lax.all_to_all(spread, 'panel', split_axis=0, concat_axis=0, tiled=True)  17.5 us
    pallas_call x1, Pallas kernels, green(): pl.pallas_call(green_kernel, out_shape=jax.ShapeDtypeStruct((2, points),...  13.5 us
    all_to_all x1, blocking collectives, shards(): lax.all_to_all(copies, 'point', split_axis=0, concat_axis=0, tiled=True)  10.8 us

profile of v5, /device:TPU:1, one launch (start us, length us, event | category | flops | bytes accessed | tf_op | source)
XLA Modules:
  0.0 73.9 jit_solution(10167581801334713044)
XLA Ops:
  0.0 0.0 copy-start.3
  0.0 0.0 copy-start.4
  0.0 0.8 %fusion.6 = f32[64,2048]{1,0:T(8,128)S(1)} fusion(s32[2048]{0:T(1024)} %bitcast.18), kind=kLoop, calls=%fused_computation.8 | loop fusion | flops 262144 | bytes 532480 | tf_op jit(solution)/shard_map/convert_element_type | solution.py:94
  0.8 0.0 copy-done.3
  0.8 0.0 copy-done.4
  0.8 0.9 %convolution_bitcast_fusion = f32[64,2,128]{2,0,1:T(8,128)S(1)} fusion(s32[2048]{0:T(1024)S(1)} %copy-done.4, f32[64,2048]{1,0:T(8,128)S(1)} %fusion.6, f32[2,2048]{1,0:T(2,128)S(1)} %copy-done.3), kind=kOutput, calls=%fused_computation | convolution fusion | flops 403177472 | bytes 614400 | tf_op jit(solution)/shard_map/dot_general | solution.py:101
  1.6 0.1 copy.9
  1.7 28.1 %all_to_all.15 = f32[64,2,128]{2,1,0:T(2,128)S(1)} all-to-all(f32[64,2,128]{2,1,0:T(2,128)S(1)} %copy.9), channel_id=1, replica_groups=mesh['panel'=64,'point'=8] {'panel'}, dimensions={0} | all-to-all | bytes 131072 | tf_op jit(solution)/shard_map/all_to_all | solution.py:105
  29.8 0.1 reduce_sum.18
  29.8 10.8 %all_to_all.16 = f32[8,2,128]{2,1,0:T(2,128)S(1)} all-to-all(f32[8,2,128]{2,1,0:T(2,128)S(1)} %broadcast_in_dim.6), channel_id=1, replica_groups=mesh['panel'=64,'point'=8] {'point'}, dimensions={0} | all-to-all | bytes 16384 | tf_op jit(solution)/shard_map/all_to_all | solution.py:109
  40.7 0.0 copy-start.2
  40.7 0.6 copy-done.2
  41.3 0.0 copy-start.1
  41.3 0.7 copy-done.1
  42.0 0.0 copy-start
  42.0 17.5 %all_to_all.17.panel_ref = f32[64,5,128]{2,1,0:T(8,128)} all-to-all(f32[64,5,128]{2,1,0:T(8,128)S(1)} %broadcast_in_dim.7), channel_id=1, replica_groups=mesh['panel'=64,'point'=8] {'panel'}, dimensions={0} | all-to-all | bytes 327680 | tf_op jit(solution)/shard_map/all_to_all | solution.py:113
  59.5 0.0 copy-done
  59.5 0.8 %broadcast_in_dim.8.point_ref = f32[3,128,128]{2,1,0:T(8,128)} broadcast(f32[3,128]{1,0:T(4,128)S(1)} %copy-done), dimensions={0,1} | broadcast | bytes 198144 | tf_op jit(solution)/shard_map/broadcast_in_dim | solution.py:78
  60.3 13.5 %shard_map.64 = f32[2,128]{1,0:T(2,128)} custom-call(f32[64,5,128]{2,1,0:T(8,128)} %all_to_all.17.panel_ref, f32[3,128,128]{2,1,0:T(8,128)} %broadcast_in_dim.8.point_ref), custom_call_target="tpu_custom_call" | custom-call | flops 73400320 | bytes 361472 | tf_op jit(solution)/shard_map/pallas_call | solution.py:80
  (5 shorter events, 0.1 us)
Async XLA Ops:
  0.0 0.8 %copy-start.3 = (f32[2,2048]{1,0:T(2,128)S(1)}, f32[2,2048]{1,0:T(2,128)}, u32[]{:S(2)}) copy-start(f32[2,2048]{1,0:T(2,128)} %param.6) | copy-start | bytes 49156
  0.0 0.8 %copy-start.4 = (s32[2048]{0:T(1024)S(1)}, s32[2048]{0:T(1024)}, u32[]{:S(2)}) copy-start(s32[2048]{0:T(1024)} %param.8) | copy-start | bytes 24580
  40.7 0.7 copy-start.2
  41.3 0.7 copy-start.1
  42.0 17.5 %copy-start = (f32[3,128]{1,0:T(4,128)S(1)}, f32[3,128]{1,0:T(4,128)}, u32[]{:S(2)}) copy-start(f32[3,128]{1,0:T(4,128)} %param.11) | copy-start | bytes 4612
